TPU v7x, 32 devices: a whole 2x2x4 slice. The times are simulated.
32 devices in a mesh: rows: 4 (over y, x), cols: 8 (over z, core).
Axes of the slice: x: 2, y: 2, z: 4, core: 2. Of those that a mesh axis runs over, the one named last changes fastest.
Arguments:
- features: bfloat16 [32, 128, 1024], P('rows', 'cols'), may hold values from -24 to 24
- w_query: bfloat16 [1024, 1024], replicated, may hold values from -0.1875 to 0.1875
- w_key: bfloat16 [1024, 1024], replicated, may hold values from -0.1875 to 0.1875
- w_value: bfloat16 [1024, 1024], replicated, may hold values from -0.1875 to 0.1875
- w_out: bfloat16 [1024, 1024], replicated, may hold values from -0.1875 to 0.1875
- reg_pos: int32 [32], replicated, may hold values from 0 to 4095, as said below
- grad_out: bfloat16 [32, 128, 1024], P('rows', 'cols'), may hold values from -6 to 6
Outputs:
- layer_out: bfloat16 [32, 128, 1024], P('rows', 'cols')
- grad_in: bfloat16 [32, 128, 1024], P('rows', 'cols')
Inputs may be any that keep to these rules, and one draw needn't show every extreme that they name: The 32 global tokens are distinct, one in each tile of 128 tokens: reg_pos[r] lies in tile row r // 8 and tile column r % 8, tiles counted row by row.
All inputs are finite; a program needn't handle non-finite values.
Results may differ from a plain program's by a relative error of at most 0.03.
The roundings to bfloat16 on the way count: a program that leaves them out, or rounds other values in their place, can miss the bound.
Values may be sent and summed in bfloat16 or wider, within the bound.
No kernel may reach another device: no remote copies, remote signals or barrier semaphores. Data moves between devices by JAX's collectives and lax.ppermute only.
A program may use at most 128 MiB of HBM per device.

v0:
```python
import math
import jax
import jax.numpy as jnp
from jax import lax
from jax.sharding import PartitionSpec as P

HEADS = 16
KW = 13
RAD = 6


def with_halo(block, sides, width):
    for axis, dim in sides:
        count = lax.axis_size(axis)
        forward = [(i, i + 1) for i in range(count - 1)]
        backward = [(target, source) for source, target in forward]
        low = lax.ppermute(
            lax.slice_in_dim(block, block.shape[dim] - width, None, axis=dim), axis, forward
        )
        high = lax.ppermute(lax.slice_in_dim(block, 0, width, axis=dim), axis, backward)
        block = jnp.concatenate([low, block, high], axis=dim)
    return block


def from_behind(x, axis, by):
    size = lax.axis_size(axis)
    pairs = [(i, i + by) for i in range(size) if 0 <= i + by < size]
    return lax.ppermute(x, axis, pairs)


def axis_valid(first_cell, tile, extent):
    query_cell = first_cell + jnp.arange(tile, dtype=jnp.int32)[:, None]
    key_cell = first_cell - RAD + jnp.arange(tile + 2 * RAD, dtype=jnp.int32)[None, :]
    window_start = jnp.clip(query_cell - RAD, 0, extent - KW)
    return (key_cell >= window_start) & (key_cell <= window_start + KW - 1)


def einsum_wide(form, left, right):
    return jnp.einsum(form, left, right, preferred_element_type=jnp.float32)


def to_heads(x):
    count, width = x.shape
    return x.reshape(count, HEADS, width // HEADS).transpose(1, 0, 2)


def from_heads(x):
    heads, count, size = x.shape
    return x.transpose(1, 0, 2).reshape(count, heads * size)


def shards(features, w_query, w_key, w_value, w_out, reg_pos, grad_out):
    tile_rows, tile_cols, model_width = features.shape
    head_size = model_width // HEADS
    score_scale = 1.0 / math.sqrt(head_size)
    row_count = lax.axis_size("rows")
    col_count = lax.axis_size("cols")
    row_index = lax.axis_index("rows")
    col_index = lax.axis_index("cols")
    band_cols = tile_cols * col_count
    first_row = row_index * tile_rows
    first_col = col_index * tile_cols
    tokens = tile_rows * tile_cols
    frame_rows = tile_rows + 2 * RAD
    frame_cols = tile_cols + 2 * RAD
    flat_tokens = features.reshape(-1, model_width)
    queries = jnp.dot(flat_tokens, w_query, preferred_element_type=jnp.float32).astype(jnp.bfloat16)
    keys_local = jnp.dot(flat_tokens, w_key, preferred_element_type=jnp.float32).astype(
        jnp.bfloat16
    )
    values_local = jnp.dot(flat_tokens, w_value, preferred_element_type=jnp.float32).astype(
        jnp.bfloat16
    )
    key_value = jnp.concatenate([keys_local, values_local], axis=1)
    own_index = row_index * col_count + col_index
    own_place = lax.dynamic_index_in_dim(reg_pos, own_index, 0, keepdims=False)
    own_local = (own_place // band_cols - first_row) * tile_cols + (
        own_place % band_cols - first_col
    )
    own_kv = lax.dynamic_slice_in_dim(key_value, own_local, 1, 0)
    global_kv = lax.all_gather(own_kv, ("rows", "cols"), axis=0, tiled=True)
    framed = with_halo(
        key_value.reshape(tile_rows, tile_cols, 2 * model_width), (("rows", 0), ("cols", 1)), RAD
    ).reshape(frame_rows * frame_cols, 2 * model_width)
    all_kv = jnp.concatenate([framed, global_kv], axis=0)
    key_count = all_kv.shape[0]
    row_valid = axis_valid(first_row, tile_rows, tile_rows * row_count)
    col_valid = axis_valid(first_col, tile_cols, band_cols)
    window_mask = (row_valid[:, None, :, None] & col_valid[None, :, None, :]).reshape(
        tokens, frame_rows * frame_cols
    )
    full_mask = jnp.concatenate(
        [window_mask, jnp.ones((tokens, key_count - frame_rows * frame_cols), jnp.bool_)], axis=1
    )
    query_heads = to_heads(queries)
    key_heads = to_heads(all_kv[:, :model_width])
    value_heads = to_heads(all_kv[:, model_width:])
    scores = einsum_wide("hqd,hkd->hqk", query_heads, key_heads) * score_scale
    scores = jnp.where(full_mask[None], scores, -1e30)
    row_max = jnp.max(scores, axis=-1, keepdims=True)
    exps = jnp.exp(scores - row_max)
    denominator = jnp.sum(exps, axis=-1, keepdims=True)
    probs = exps / denominator
    rounded = probs.astype(jnp.bfloat16)
    attended_heads = einsum_wide("hqk,hkd->hqd", rounded, value_heads).astype(jnp.bfloat16)
    attended = from_heads(attended_heads)
    layer_out = (
        jnp.dot(attended, w_out, preferred_element_type=jnp.float32)
        .astype(jnp.bfloat16)
        .reshape(features.shape)
    )
    grad_attended = jnp.dot(
        grad_out.reshape(-1, model_width), w_out.T, preferred_element_type=jnp.float32
    ).astype(jnp.bfloat16)
    grad_heads = to_heads(grad_attended)
    delta = einsum_wide("hqd,hqd->hq", grad_heads, attended_heads)[..., None]
    dots = einsum_wide("hqd,hkd->hqk", grad_heads, value_heads)
    slopes = (probs * (dots - delta) * score_scale).astype(jnp.bfloat16)
    query_grads = from_heads(einsum_wide("hqk,hkd->hqd", slopes, key_heads).astype(jnp.bfloat16))
    key_grads = from_heads(einsum_wide("hqk,hqd->hkd", slopes, query_heads))
    value_grads = from_heads(einsum_wide("hqk,hqd->hkd", rounded, grad_heads))
    kv_grads_all = jnp.concatenate([key_grads, value_grads], axis=1)
    global_grads = kv_grads_all[frame_rows * frame_cols :]
    own_grads = lax.psum_scatter(global_grads, ("rows", "cols"), scatter_dimension=0, tiled=True)
    frame_grads = kv_grads_all[: frame_rows * frame_cols].reshape(
        frame_rows, frame_cols, 2 * model_width
    )
    left_rim = frame_grads[:, :RAD]
    right_rim = frame_grads[:, tile_cols + RAD :]
    centre = frame_grads[:, RAD : tile_cols + RAD]
    from_right = from_behind(left_rim.astype(jnp.bfloat16), "cols", -1).astype(left_rim.dtype)
    from_left = from_behind(right_rim.astype(jnp.bfloat16), "cols", 1).astype(right_rim.dtype)
    centre = centre.at[:, tile_cols - RAD :].add(from_right).at[:, :RAD].add(from_left)
    upper_rim = centre[:RAD]
    lower_rim = centre[tile_rows + RAD :]
    middle = centre[RAD : tile_rows + RAD]
    from_below = from_behind(upper_rim.astype(jnp.bfloat16), "rows", -1).astype(upper_rim.dtype)
    from_above = from_behind(lower_rim.astype(jnp.bfloat16), "rows", 1).astype(lower_rim.dtype)
    middle = middle.at[tile_rows - RAD :].add(from_below).at[:RAD].add(from_above)
    middle = middle.reshape(tokens, 2 * model_width)
    own_row = lax.dynamic_slice_in_dim(middle, own_local, 1, 0) + own_grads
    kv_grads = lax.dynamic_update_slice_in_dim(middle, own_row, own_local, 0).astype(jnp.bfloat16)
    grad_in = (
        jnp.dot(query_grads, w_query.T, preferred_element_type=jnp.float32)
        + jnp.dot(kv_grads[:, :model_width], w_key.T, preferred_element_type=jnp.float32)
        + jnp.dot(kv_grads[:, model_width:], w_value.T, preferred_element_type=jnp.float32)
    )
    grad_in = grad_in.astype(jnp.bfloat16).reshape(features.shape)
    return (layer_out, grad_in)


def solution(mesh):
    placed = (P("rows", "cols", None), P(), P(), P(), P(), P(), P("rows", "cols", None))
    return jax.shard_map(
        shards,
        mesh=mesh,
        in_specs=placed,
        out_specs=(P("rows", "cols", None), P("rows", "cols", None)),
        check_vma=False,
    )
```

profile of v0, /device:TPU:0, one launch (start us, length us, event | category | flops | bytes accessed | tf_op | source)
XLA Modules:
  0.0 321.7 jit_solution(17571939604907091626)
XLA Ops:
  7.2 2.3 convolution_convert_fusion.4
  9.7 0.4 convolution_convert_fusion.5
  10.2 1.1 copy.41
  11.3 5.6 %collective-permute-start = (bf16[6,16,2048]{2,0,1:T(8,128)(2,1)}, bf16[6,16,2048]{2,0,1:T(8,128)(2,1)}, u32[]{:S(2)}, u32[]{:S(2)}) collective-permute-start(bf16[6,16,2048]{2,0,1:T(8,128)(2,1)} %copy.41), channel_id=1, source_target_pairs={{0,8},{8,16},{16,24},{1,9},{9,17},{17,25},{2,10},{10,18},{18,26},{... | collective-permute-start | bytes 1179656 | tf_op jit(solution)/shard_map/ppermute | solution.py:17
  16.9 1.0 copy.42
  18.0 1.3 collective-permute-start.1
  19.3 0.6 dynamic_slice.10
  22.6 2.8 convolution_convert_fusion.6
  25.4 0.3 copy.43
  25.8 0.8 convolution_convert_fusion.2
  26.7 1.0 collective-permute-done
  27.6 13.2 %collective-permute-done.1 = bf16[6,16,2048]{2,0,1:T(8,128)(2,1)} collective-permute-done((bf16[6,16,2048]{2,0,1:T(8,128)(2,1)}, bf16[6,16,2048]{2,0,1:T(8,128)(2,1)}, u32[]{:S(2)}, u32[]{:S(2)}) %collective-permute-start.1) | collective-permute-done | bytes 393248 | tf_op jit(solution)/shard_map/ppermute | solution.py:20
  40.8 2.7 pad_maximum_fusion.5
  43.5 2.1 collective-permute-start.2
  45.6 1.3 collective-permute-start.3
  46.9 43.1 %all-gather = bf16[32,1,2048]{2,1,0:T(2,128)(2,1)S(1)} all-gather(bf16[1,1,2048]{2,1,0:T(2,128)(2,1)S(1)} %fusion.19), channel_id=1, replica_groups=mesh['rows'=4,'cols'=8] {'rows','cols'}, dimensions={0}, use_global_device_ids=true | all-gather | bytes 135168 | tf_op jit(solution)/shard_map/all_gather | solution.py:81
  90.0 0.8 copy.40
  90.9 0.8 copy.47
  91.8 0.2 broadcast_and_fusion
  92.1 0.5 and.60
  92.8 2.4 pad_maximum_fusion
  95.2 2.8 copy.44
  98.0 4.0 %reshape.324 = bf16[560,2048]{1,0:T(8,128)(2,1)} reshape(bf16[20,28,2048]{2,1,0:T(8,128)(2,1)} %copy.44) | data formatting | bytes 4587520 | tf_op jit(solution)/shard_map/reshape | solution.py:84
  102.0 3.3 %pad_maximum_fusion.1 = (bf16[592,1024]{1,0:T(8,128)(2,1)}, bf16[592,1024]{1,0:T(8,128)(2,1)}) fusion(bf16[32,2048]{1,0:T(8,128)(2,1)S(1)} %bitcast.90, bf16[560,2048]{1,0:T(8,128)(2,1)} %reshape.324), kind=kLoop, calls=%fused_computation.21 | loop fusion | flops 4849664 | bytes 4849664 | tf_op jit(solution)/shard_map/concatenate | solution.py:85
  105.2 1.7 copy.45
  106.9 2.4 copy.46
  109.4 5.0 %fusion.24 = (f32[16,128]{1,0:T(8,128)S(1)}, f32[16,128,592]{1,2,0:T(8,128)}) fusion(pred[128,592]{0,1:T(8,128)(4,1)S(1)} %concatenate.26.clone, bf16[16,128,64]{1,2,0:T(8,128)(2,1)} %bitcast.87, bf16[16,592,64]{1,2,0:T(8,128)(2,1)S(1)} %bitcast.72), kind=kOutput, calls=%fused_computation.69 | convolution fusion | flops 160039504 | bytes 6408192 | tf_op jit(solution)/shard_map/sub | solution.py:101
  114.4 2.9 fusion.6
  117.3 1.3 fusion.11
  118.6 2.4 fusion.27
  121.0 1.3 multiply_convert_fusion
  122.4 2.4 fusion.26
  124.9 3.2 copy.49
  128.1 3.2 copy.48
  131.3 5.0 %fusion.1 = f32[560,2048]{1,0:T(8,128)} fusion(f32[592,1024]{1,0:T(8,128)} %copy.48, f32[592,1024]{1,0:T(8,128)} %copy.49), kind=kLoop, calls=%fused_computation.6 | loop fusion | flops 1146880 | bytes 9437184 | tf_op jit(solution)/shard_map/concatenate | solution.py:122
  136.3 5.4 %reshape.334 = f32[20,28,2048]{2,1,0:T(8,128)} reshape(f32[560,2048]{1,0:T(8,128)} %fusion.1) | data formatting | bytes 9175040 | tf_op jit(solution)/shard_map/reshape | solution.py:125
  141.7 3.0 convert.8
  144.7 1.0 copy-done.1
  145.8 2.0 slice.186
  147.7 0.3 fusion.22
  148.0 1.1 copy.52
  149.1 0.3 copy.50
  149.4 1.3 collective-permute-start.4
  150.7 3.9 %collective-permute-start.5 = (bf16[20,6,2048]{2,0,1:T(8,128)(2,1)}, bf16[20,6,2048]{2,0,1:T(8,128)(2,1)}, u32[]{:S(2)}, u32[]{:S(2)}) collective-permute-start(bf16[20,6,2048]{2,0,1:T(8,128)(2,1)} %copy.52), channel_id=1, source_target_pairs={{0,1},{1,2},{2,3},{3,4},{4,5},{5,6},{6,7},{8,9},{9,10},{10,11},{11... | collective-permute-start | bytes 1474568 | tf_op jit(solution)/shard_map/ppermute | solution.py:28
  154.6 1.2 convolution_convert_fusion.3
  155.7 1.4 convolution_convert_fusion
  157.1 0.4 slice_add_fusion.1
  157.5 6.2 %scatter-add.14 = f32[20,16,2048]{2,1,0:T(8,128)} dynamic-update-slice(f32[20,16,2048]{2,1,0:T(8,128)} %slice.186, f32[20,6,2048]{2,1,0:T(8,128)S(1)} %slice_add_fusion.1, s32[]{:T(128)} %constant.163.clone.1, s32[]{:T(128)} %constant.180.clone.1, s32[]{:T(128)} %constant.163.clone.1) | dynamic-update-slice | bytes 1966084 | tf_op jit(solution)/shard_map/scatter-add | solution.py:133
  163.7 1.8 slice_add_fusion
  165.5 7.0 %scatter-add.15 = f32[20,16,2048]{2,1,0:T(8,128)} dynamic-update-slice(f32[20,16,2048]{2,1,0:T(8,128)} %scatter-add.14, f32[20,6,2048]{2,1,0:T(8,128)S(1)} %slice_add_fusion, s32[]{:T(128)} %constant.163.clone.1, s32[]{:T(128)} %constant.163.clone.1, s32[]{:T(128)} %constant.163.clone.1) | dynamic-update-slice | bytes 1966084 | tf_op jit(solution)/shard_map/scatter-add | solution.py:133
  172.5 2.1 convert.9
  174.6 0.8 fusion.23
  175.4 1.4 collective-permute-start.6
  176.9 0.7 pad_maximum_fusion.6
  177.6 3.4 %fusion.25 = f32[128,1024]{1,0:T(8,128)} fusion(bf16[128,1024]{0,1:T(8,128)(2,1)S(1)} %bitcast.89, bf16[1024,1024]{1,0:T(8,128)(2,1)} %param.16), kind=kOutput, calls=%fused_computation.70 | convolution fusion | flops 268435456 | bytes 2883584 | tf_op jit(solution)/shard_map/dot_general | solution.py:144
  181.1 4.6 %collective-permute-start.7 = (bf16[6,16,2048]{2,1,0:T(8,128)(2,1)S(1)}, bf16[6,16,2048]{2,1,0:T(8,128)(2,1)S(1)}, u32[]{:S(2)}, u32[]{:S(2)}) collective-permute-start(bf16[6,16,2048]{2,1,0:T(8,128)(2,1)S(1)} %get-tuple-element.56), channel_id=1, source_target_pairs={{0,8},{8,16},{16,24},{1,9},{9,17},{17,25},{2,10},{10,18},{18,26},{... | collective-permute-start | bytes 1179656 | tf_op jit(solution)/shard_map/ppermute | solution.py:28
  185.7 1.1 collective-permute-done.6
  186.8 1.1 fusion.10
  187.9 4.8 %collective-permute-done.7 = bf16[6,16,2048]{2,1,0:T(8,128)(2,1)S(1)} collective-permute-done((bf16[6,16,2048]{2,1,0:T(8,128)(2,1)S(1)}, bf16[6,16,2048]{2,1,0:T(8,128)(2,1)S(1)}, u32[]{:S(2)}, u32[]{:S(2)}) %collective-permute-start.7) | collective-permute-done | bytes 393248 | tf_op jit(solution)/shard_map/ppermute | solution.py:28
  192.9 116.6 %all-reduce.4.cloned.1.call-done = f32[32,2048]{1,0:T(8,128)} async-done(((f32[32,2048]{1,0:T(8,128)}), f32[32,2048]{1,0:T(8,128)}) %all-reduce.4.cloned.1.call-update) | async-done | bytes 262160
  309.5 0.9 dynamic-slice_add_fusion
  310.4 0.2 dynamic_update_slice.3
  310.7 2.6 convolution_add_fusion.1
  313.3 1.5 fusion.8
  (61 shorter events, 1.2 us)
Async XLA Ops:
  7.2 18.6 %copy-start = (bf16[1024,1024]{1,0:T(8,128)(2,1)S(1)}, bf16[1024,1024]{1,0:T(8,128)(2,1)}, u32[]{:S(2)}) copy-start(bf16[1024,1024]{1,0:T(8,128)(2,1)} %param.19) | copy-start | bytes 6291460
  7.2 2.3 copy-start.10
  7.2 302.3 %all-reduce.4.cloned.1.call-start = ((), (), s32[]{:S(2)}) async-start(), calls=%async_computation | async-start | bytes 524288
  7.2 2.5 copy-start.8
  9.7 9.6 %copy-start.17 = (s32[32]{0:T(128)S(1)}, s32[32]{0:T(128)}, u32[]{:S(2)}) copy-start(s32[32]{0:T(128)} %param.20) | copy-start | bytes 388
  11.3 16.3 %collective-permute-start = (bf16[6,16,2048]{2,0,1:T(8,128)(2,1)}, bf16[6,16,2048]{2,0,1:T(8,128)(2,1)}, u32[]{:S(2)}, u32[]{:S(2)}) collective-permute-start(bf16[6,16,2048]{2,0,1:T(8,128)(2,1)} %copy.41), channel_id=1, source_target_pairs={{0,8},{8,16},{16,24},{1,9},{9,17},{17,25},{2,10},{10,18},{18,26},{... | collective-permute-start | bytes 1179656 | tf_op jit(solution)/shard_map/ppermute | solution.py:17
  18.0 22.8 %collective-permute-start.1 = (bf16[6,16,2048]{2,0,1:T(8,128)(2,1)}, bf16[6,16,2048]{2,0,1:T(8,128)(2,1)}, u32[]{:S(2)}, u32[]{:S(2)}) collective-permute-start(bf16[6,16,2048]{2,0,1:T(8,128)(2,1)} %copy.42), channel_id=1, source_target_pairs={{8,0},{16,8},{24,16},{9,1},{17,9},{25,17},{10,2},{18,10},{26,18},{... | collective-permute-start | bytes 1179656 | tf_op jit(solution)/shard_map/ppermute | solution.py:20
  22.6 3.2 copy-start.16
  25.8 64.2 %copy-start.13 = (bf16[128,1024]{1,0:T(8,128)(2,1)S(1)}, bf16[128,1024]{1,0:T(8,128)(2,1)}, u32[]{:S(2)}) copy-start(bf16[128,1024]{1,0:T(8,128)(2,1)} %convolution_convert_fusion.6) | copy-start | bytes 786436
  43.5 49.3 %collective-permute-start.2 = (bf16[20,6,2048]{2,0,1:T(8,128)(2,1)}, bf16[20,6,2048]{2,0,1:T(8,128)(2,1)}, u32[]{:S(2)}, u32[]{:S(2)}) collective-permute-start(bf16[20,6,2048]{2,0,1:T(8,128)(2,1)} %get-tuple-element.54), channel_id=1, source_target_pairs={{0,1},{1,2},{2,3},{3,4},{4,5},{5,6},{6,7},{8,9},{9,10},{10,11},{11... | collective-permute-start | bytes 1474568 | tf_op jit(solution)/shard_map/ppermute | solution.py:17
  45.6 47.2 %collective-permute-start.3 = (bf16[20,6,2048]{2,0,1:T(8,128)(2,1)}, bf16[20,6,2048]{2,0,1:T(8,128)(2,1)}, u32[]{:S(2)}, u32[]{:S(2)}) collective-permute-start(bf16[20,6,2048]{2,0,1:T(8,128)(2,1)} %get-tuple-element.55), channel_id=1, source_target_pairs={{1,0},{2,1},{3,2},{4,3},{5,4},{6,5},{7,6},{9,8},{10,9},{11,10},{12... | collective-permute-start | bytes 1474568 | tf_op jit(solution)/shard_map/ppermute | solution.py:20
  114.4 2.9 copy-start.9
  114.4 2.9 copy-start.11
  114.4 6.7 %slice-start = ((s8[4849664]{0:T(1024)(128)(4,1)}), s8[4194304]{0:T(1024)(128)(4,1)S(1)}, s32[]{:S(2)}) async-start(s8[4849664]{0:T(1024)(128)(4,1)} %bitcast.76), calls=%async_computation.1 | async-start | bytes 8388608
  117.3 3.8 %slice-start.1 = ((s8[4849664]{0:T(1024)(128)(4,1)}), s8[655360]{0:T(1024)(128)(4,1)S(1)}, s32[]{:S(2)}) async-start(s8[4849664]{0:T(1024)(128)(4,1)} %bitcast.76), calls=%async_computation.2 | async-start | bytes 1310720
  121.0 1.4 copy-start.14
  122.4 2.4 copy-start.5
  141.7 4.0 %copy-start.1 = (f32[20,28,2048]{2,1,0:T(8,128)S(1)}, f32[20,28,2048]{2,1,0:T(8,128)}, u32[]{:S(2)}) copy-start(f32[20,28,2048]{2,1,0:T(8,128)} %reshape.334) | copy-start | bytes 13762564
  147.7 6.8 %copy-start.12 = (bf16[16,128,64]{1,2,0:T(8,128)(2,1)S(1)}, bf16[16,128,64]{1,2,0:T(8,128)(2,1)}, u32[]{:S(2)}) copy-start(bf16[16,128,64]{1,2,0:T(8,128)(2,1)} %get-tuple-element.63) | copy-start | bytes 786436
  148.0 7.7 %copy-start.6 = (bf16[16,128,592]{1,2,0:T(8,128)(2,1)S(1)}, bf16[16,128,592]{1,2,0:T(8,128)(2,1)}, u32[]{:S(2)}) copy-start(bf16[16,128,592]{1,2,0:T(8,128)(2,1)} %copy-done.5) | copy-start | bytes 7274500
  149.4 7.7 %collective-permute-start.4 = (bf16[20,6,2048]{2,0,1:T(8,128)(2,1)S(1)}, bf16[20,6,2048]{2,0,1:T(8,128)(2,1)S(1)}, u32[]{:S(2)}, u32[]{:S(2)}) collective-permute-start(bf16[20,6,2048]{2,0,1:T(8,128)(2,1)S(1)} %copy.50), channel_id=1, source_target_pairs={{1,0},{2,1},{3,2},{4,3},{5,4},{6,5},{7,6},{9,8},{10,9},{11,10},{12... | collective-permute-start | bytes 1474568 | tf_op jit(solution)/shard_map/ppermute | solution.py:28
  150.7 13.0 %collective-permute-start.5 = (bf16[20,6,2048]{2,0,1:T(8,128)(2,1)}, bf16[20,6,2048]{2,0,1:T(8,128)(2,1)}, u32[]{:S(2)}, u32[]{:S(2)}) collective-permute-start(bf16[20,6,2048]{2,0,1:T(8,128)(2,1)} %copy.52), channel_id=1, source_target_pairs={{0,1},{1,2},{2,3},{3,4},{4,5},{5,6},{6,7},{8,9},{9,10},{10,11},{11... | collective-permute-start | bytes 1474568 | tf_op jit(solution)/shard_map/ppermute | solution.py:28
  172.5 4.3 %copy-start.3 = (f32[592,1024]{1,0:T(8,128)S(1)}, f32[592,1024]{1,0:T(8,128)}, u32[]{:S(2)}) copy-start(f32[592,1024]{1,0:T(8,128)} %copy.49) | copy-start | bytes 7274500
  172.5 4.3 %copy-start.4 = (f32[592,1024]{1,0:T(8,128)S(1)}, f32[592,1024]{1,0:T(8,128)}, u32[]{:S(2)}) copy-start(f32[592,1024]{1,0:T(8,128)} %copy.48) | copy-start | bytes 7274500
  175.4 2.2 copy-start.15
  175.4 11.4 %collective-permute-start.6 = (bf16[6,16,2048]{2,1,0:T(8,128)(2,1)}, bf16[6,16,2048]{2,1,0:T(8,128)(2,1)}, u32[]{:S(2)}, u32[]{:S(2)}) collective-permute-start(bf16[6,16,2048]{2,1,0:T(8,128)(2,1)} %get-tuple-element.57), channel_id=1, source_target_pairs={{8,0},{16,8},{24,16},{9,1},{17,9},{25,17},{10,2},{18,10},{26,18},{... | collective-permute-start | bytes 1179656 | tf_op jit(solution)/shard_map/ppermute | solution.py:28
  177.6 3.4 %copy-start.2 = (f32[20,16,2048]{2,1,0:T(8,128)S(1)}, f32[20,16,2048]{2,1,0:T(8,128)}, u32[]{:S(2)}) copy-start(f32[20,16,2048]{2,1,0:T(8,128)} %scatter-add.15) | copy-start | bytes 7864324
  181.1 11.6 %collective-permute-start.7 = (bf16[6,16,2048]{2,1,0:T(8,128)(2,1)S(1)}, bf16[6,16,2048]{2,1,0:T(8,128)(2,1)S(1)}, u32[]{:S(2)}, u32[]{:S(2)}) collective-permute-start(bf16[6,16,2048]{2,1,0:T(8,128)(2,1)S(1)} %get-tuple-element.56), channel_id=1, source_target_pairs={{0,8},{8,16},{16,24},{1,9},{9,17},{17,25},{2,10},{10,18},{18,26},{... | collective-permute-start | bytes 1179656 | tf_op jit(solution)/shard_map/ppermute | solution.py:28
  310.6 2.7 copy-start.7
Sparse Core Ops, SparseCore 0:
  177.7 131.7 all-reduce.3
where the time goes:
time: 323 us; the launch traced here: 322 us
  waiting for transfers between devices  137 us (42%)
  local copies, waits for them, and re-layouts  47.4 us (15%)
  blocking collectives  43.1 us (13%)
  matrix products  28.9 us (9%)
  other arithmetic  27 us (8%)
  starting transfers between devices  21.5 us (7%)
  between operations  17.1 us (5%)
    unnamed x2, waiting for transfers between devices  117 us
    all_gather x1, blocking collectives, shards(): global_kv = lax.all_gather(own_kv, ('rows', 'cols'), axis=0, tiled=True)  43.1 us
    scatter-add x2, local copies, waits for them, and re-layouts, shards(): centre.at[:, tile_cols - RAD:].add(from_right).at[:, :RAD].add(from_left)  13.2 us
    ppermute x2, waiting for transfers between devices, with_halo(): lax.ppermute(lax.slice_in_dim(block, 0, width, axis=dim), axis, backward)  13.2 us
    ppermute x4, starting transfers between devices, from_behind(): return lax.ppermute(x, axis, pairs)  11.1 us
    dot_general x5, matrix products, einsum_wide(): return jnp.einsum(form, left, right, preferred_element_type=jnp.float32)  8.87 us
    ppermute x2, starting transfers between devices, with_halo(): lax.ppermute(lax.slice_in_dim(block, block.shape[dim] - width, None, axis...  7.75 us
  transfers between devices with their start and end apart: 9, of which 5 were waited for; matrix products, arithmetic and copies ran while one was open for 7% of the time, Pallas kernels for 0%

commit v1 on v0

--- a/solution.py
+++ b/solution.py
@@ -7,6 +7,28 @@
 HEADS = 16
 KW = 13
 RAD = 6
+
+
+def in_order(pieces, dim):
+    pieces = jnp.moveaxis(pieces, 0, dim)
+    lengths = pieces.shape
+    return pieces.reshape(*lengths[:dim], lengths[dim] * lengths[dim + 1], *lengths[dim + 2 :])
+
+
+def grow_blocks(shard, axis):
+    devices = lax.axis_size(axis)
+    blocks = shard[None]
+    for level in range(devices.bit_length() - 1):
+        distance = 1 << level
+        partner_block = lax.ppermute(blocks, axis, [(i, i ^ distance) for i in range(devices)])
+        both = jnp.stack([blocks, partner_block])
+        upper = lax.axis_index(axis) >> level & 1
+        blocks = jnp.where(upper == 0, both, both[::-1]).reshape(-1, *shard.shape)
+    return blocks
+
+
+def gather_by_bits(array, axis, dim):
+    return in_order(grow_blocks(array, axis), dim)
 
 
 def with_halo(block, sides, width):
@@ -78,7 +100,7 @@
         own_place % band_cols - first_col
     )
     own_kv = lax.dynamic_slice_in_dim(key_value, own_local, 1, 0)
-    global_kv = lax.all_gather(own_kv, ("rows", "cols"), axis=0, tiled=True)
+    global_kv = gather_by_bits(own_kv, ("rows", "cols"), 0)
     framed = with_halo(
         key_value.reshape(tile_rows, tile_cols, 2 * model_width), (("rows", 0), ("cols", 1)), RAD
     ).reshape(frame_rows * frame_cols, 2 * model_width)

time: 323 us -> 291 us (0.901)
  blocking collectives: 43.1 us -> 0 us
  starting transfers between devices: 21.5 us -> 35.8 us
  waiting for transfers between devices: 137 us -> 133 us
    all_gather x1 -> x0, blocking collectives: 43.1 us -> none  [shards(): global_kv = lax.all_gather(own_kv, ('rows', 'cols'), axis=0, tiled=True)]
    ppermute x2, waiting for transfers between devices: 13.2 us -> 3.67 us  [with_halo(): lax.ppermute(lax.slice_in_dim(block, 0, width, axis=dim), axis, backward)]
    ppermute x0 -> x5, starting transfers between devices: none -> 7.6 us  [grow_blocks(): lax.ppermute(blocks, axis, [(i, i ^ distance) for i in range(devices)])]
    ppermute x4, starting transfers between devices: 11.1 us -> 18.4 us  [from_behind(): return lax.ppermute(x, axis, pairs)]
    ppermute x0 -> x5, waiting for transfers between devices: none -> 6.83 us  [grow_blocks(): lax.ppermute(blocks, axis, [(i, i ^ distance) for i in range(devices)])]
  transfers between devices with their start and end apart: 9 -> 14, of which waited for: 5 -> 7; matrix products, arithmetic and copies ran while one was open for 7% -> 9% of each run, Pallas kernels for 0% -> 0%
where the time goes in v1:
time: 291 us; the launch traced here: 290 us
  waiting for transfers between devices  133 us (46%)
  local copies, waits for them, and re-layouts  48.7 us (17%)
  starting transfers between devices  35.8 us (12%)
  matrix products  29.8 us (10%)
  other arithmetic  25.8 us (9%)
  between operations  17.2 us (6%)
    unnamed x2, waiting for transfers between devices  117 us
    ppermute x4, starting transfers between devices, from_behind(): return lax.ppermute(x, axis, pairs)  18.4 us
    scatter-add x2, local copies, waits for them, and re-layouts, shards(): centre.at[:, tile_cols - RAD:].add(from_right).at[:, :RAD].add(from_left)  13.2 us
    dot_general x5, matrix products, einsum_wide(): return jnp.einsum(form, left, right, preferred_element_type=jnp.float32)  8.84 us
    ppermute x5, starting transfers between devices, grow_blocks(): lax.ppermute(blocks, axis, [(i, i ^ distance) for i in range(devices)])  7.6 us
    ppermute x2, starting transfers between devices, with_halo(): lax.ppermute(lax.slice_in_dim(block, block.shape[dim] - width, None, axis...  6.95 us
    ppermute x5, waiting for transfers between devices, grow_blocks(): lax.ppermute(blocks, axis, [(i, i ^ distance) for i in range(devices)])  6.83 us
    reshape x2, local copies, waits for them, and re-layouts, from_heads(): return x.transpose(1, 0, 2).reshape(count, heads * size)  6.35 us
  transfers between devices with their start and end apart: 14, of which 7 were waited for; matrix products, arithmetic and copies ran while one was open for 9% of the time, Pallas kernels for 0%

profile of v1, /device:TPU:0, one launch (start us, length us, event | category | flops | bytes accessed | tf_op | source)
XLA Modules:
  0.0 290.1 jit_solution(10839609557409828526)
XLA Ops:
  7.2 1.4 dynamic_slice.10
  11.3 2.3 convolution_convert_fusion.4
  13.6 0.4 convolution_convert_fusion.5
  14.1 0.5 collective-permute-start.4
  14.7 1.0 copy.42
  15.7 5.2 %collective-permute-start = (bf16[6,16,2048]{2,0,1:T(8,128)(2,1)}, bf16[6,16,2048]{2,0,1:T(8,128)(2,1)}, u32[]{:S(2)}, u32[]{:S(2)}) collective-permute-start(bf16[6,16,2048]{2,0,1:T(8,128)(2,1)} %copy.42), channel_id=1, source_target_pairs={{0,8},{8,16},{16,24},{1,9},{9,17},{17,25},{2,10},{10,18},{18,26},{... | collective-permute-start | bytes 1179656 | tf_op jit(solution)/shard_map/ppermute | solution.py:39
  20.9 1.0 copy.43
  21.9 1.3 collective-permute-start.1
  23.3 2.7 convolution_convert_fusion.6
  26.0 1.8 convolution_convert_fusion.2
  28.0 1.6 collective-permute-start.5
  29.6 2.1 collective-permute-done.5
  31.8 2.7 collective-permute-start.6
  34.5 2.0 collective-permute-done.6
  36.6 2.7 collective-permute-start.7
  39.5 1.8 copy.41
  41.3 0.8 copy.48
  42.2 0.5 and.75
  43.2 2.8 collective-permute-done.7
  46.1 1.7 pad_maximum_fusion.5
  47.8 1.8 collective-permute-start.2
  49.6 1.5 collective-permute-start.3
  51.2 3.7 %collective-permute-done.3 = bf16[20,6,2048]{2,0,1:T(8,128)(2,1)S(1)} collective-permute-done((bf16[20,6,2048]{2,0,1:T(8,128)(2,1)S(1)}, bf16[20,6,2048]{2,0,1:T(8,128)(2,1)S(1)}, u32[]{:S(2)}, u32[]{:S(2)}) %collective-permute-start.3) | collective-permute-done | bytes 491552 | tf_op jit(solution)/shard_map/ppermute | solution.py:42
  54.8 2.0 pad_maximum_fusion
  56.8 2.8 copy.45
  59.6 4.0 %reshape.336 = bf16[560,2048]{1,0:T(8,128)(2,1)} reshape(bf16[20,28,2048]{2,1,0:T(8,128)(2,1)} %copy.45) | data formatting | bytes 4587520 | tf_op jit(solution)/shard_map/reshape | solution.py:106
  63.6 3.2 %pad_maximum_fusion.1 = (bf16[592,1024]{1,0:T(8,128)(2,1)}, bf16[592,1024]{1,0:T(8,128)(2,1)}) fusion(bf16[32,2048]{1,0:T(8,128)(2,1)S(1)} %bitcast.110, bf16[560,2048]{1,0:T(8,128)(2,1)} %reshape.336), kind=kLoop, calls=%fused_computation.21 | loop fusion | flops 4849664 | bytes 4849664 | tf_op jit(solution)/shard_map/concatenate | solution.py:107
  66.9 1.7 copy.46
  68.6 2.4 copy.47
  71.0 5.0 %fusion.25 = (f32[16,128]{1,0:T(8,128)S(1)}, f32[16,128,592]{1,2,0:T(8,128)}) fusion(pred[128,592]{0,1:T(8,128)(4,1)S(1)} %concatenate.26.clone, bf16[16,128,64]{1,2,0:T(8,128)(2,1)} %bitcast.107, bf16[16,592,64]{1,2,0:T(8,128)(2,1)S(1)} %bitcast.92), kind=kOutput, calls=%fused_computation.81 | convolution fusion | flops 160039504 | bytes 6408192 | tf_op jit(solution)/shard_map/sub | solution.py:123
  76.0 2.9 %fusion.6 = bf16[16,128,592]{1,2,0:T(8,128)(2,1)S(1)} fusion(f32[16,128,592]{1,2,0:T(8,128)} %get-tuple-element.65, f32[16,128]{1,0:T(8,128)S(1)} %get-tuple-element.64), kind=kLoop, calls=%fused_computation.15 | loop fusion | flops 2424832 | bytes 7282688 | tf_op jit(solution)/shard_map/convert_element_type | solution.py:126
  78.9 1.3 fusion.11
  80.3 2.4 fusion.28
  82.7 1.3 multiply_convert_fusion
  84.0 2.4 fusion.27
  86.5 3.2 %copy.50 = f32[592,1024]{1,0:T(8,128)} copy(f32[592,1024]{0,1:T(8,128)} %bitcast.88) | data formatting | bytes 4849664 | tf_op jit(solution)/shard_map/reshape | solution.py:71
  89.6 3.2 %copy.49 = f32[592,1024]{1,0:T(8,128)} copy(f32[592,1024]{0,1:T(8,128)} %bitcast.89) | data formatting | bytes 4849664 | tf_op jit(solution)/shard_map/reshape | solution.py:71
  92.8 5.0 %fusion.1 = f32[560,2048]{1,0:T(8,128)} fusion(f32[592,1024]{1,0:T(8,128)} %copy.49, f32[592,1024]{1,0:T(8,128)} %copy.50), kind=kLoop, calls=%fused_computation.6 | loop fusion | flops 1146880 | bytes 9437184 | tf_op jit(solution)/shard_map/concatenate | solution.py:144
  97.8 5.4 %reshape.350 = f32[20,28,2048]{2,1,0:T(8,128)} reshape(f32[560,2048]{1,0:T(8,128)} %fusion.1) | data formatting | bytes 9175040 | tf_op jit(solution)/shard_map/reshape | solution.py:147
  103.2 3.0 %convert.8 = bf16[20,28,2048]{2,1,0:T(8,128)(2,1)S(1)} convert(f32[20,28,2048]{2,1,0:T(8,128)} %reshape.350) | non-fusion elementwise | flops 1146880 | bytes 6881280 | tf_op jit(solution)/shard_map/convert.3
  106.3 1.0 copy-done.1
  107.3 2.0 slice.186
  109.5 1.1 copy.53
  110.9 1.3 collective-permute-start.9
  112.2 11.2 %collective-permute-start.10 = (bf16[20,6,2048]{2,0,1:T(8,128)(2,1)}, bf16[20,6,2048]{2,0,1:T(8,128)(2,1)}, u32[]{:S(2)}, u32[]{:S(2)}) collective-permute-start(bf16[20,6,2048]{2,0,1:T(8,128)(2,1)} %copy.53), channel_id=1, source_target_pairs={{0,1},{1,2},{2,3},{3,4},{4,5},{5,6},{6,7},{8,9},{9,10},{10,11},{11... | collective-permute-start | bytes 1474568 | tf_op jit(solution)/shard_map/ppermute | solution.py:50
  123.4 1.2 convolution_convert_fusion.3
  124.6 1.4 convolution_convert_fusion
  125.9 0.4 slice_add_fusion.1
  126.3 6.2 %scatter-add.14 = f32[20,16,2048]{2,1,0:T(8,128)} dynamic-update-slice(f32[20,16,2048]{2,1,0:T(8,128)} %slice.186, f32[20,6,2048]{2,1,0:T(8,128)S(1)} %slice_add_fusion.1, s32[]{:T(128)} %constant.167.clone.1, s32[]{:T(128)} %constant.187.clone.1, s32[]{:T(128)} %constant.167.clone.1) | dynamic-update-slice | bytes 1966084 | tf_op jit(solution)/shard_map/scatter-add | solution.py:155
  132.5 1.8 slice_add_fusion
  134.3 7.0 %scatter-add.15 = f32[20,16,2048]{2,1,0:T(8,128)} dynamic-update-slice(f32[20,16,2048]{2,1,0:T(8,128)} %scatter-add.14, f32[20,6,2048]{2,1,0:T(8,128)S(1)} %slice_add_fusion, s32[]{:T(128)} %constant.167.clone.1, s32[]{:T(128)} %constant.167.clone.1, s32[]{:T(128)} %constant.167.clone.1) | dynamic-update-slice | bytes 1966084 | tf_op jit(solution)/shard_map/scatter-add | solution.py:155
  141.3 2.1 convert.9
  143.3 0.8 fusion.24
  144.1 1.4 collective-permute-start.11
  145.6 0.7 pad_maximum_fusion.6
  146.3 3.4 %fusion.26 = f32[128,1024]{1,0:T(8,128)} fusion(bf16[128,1024]{0,1:T(8,128)(2,1)S(1)} %bitcast.109, bf16[1024,1024]{1,0:T(8,128)(2,1)} %param.16), kind=kOutput, calls=%fused_computation.82 | convolution fusion | flops 268435456 | bytes 2883584 | tf_op jit(solution)/shard_map/dot_general | solution.py:166
  149.8 4.6 %collective-permute-start.12 = (bf16[6,16,2048]{2,1,0:T(8,128)(2,1)S(1)}, bf16[6,16,2048]{2,1,0:T(8,128)(2,1)S(1)}, u32[]{:S(2)}, u32[]{:S(2)}) collective-permute-start(bf16[6,16,2048]{2,1,0:T(8,128)(2,1)S(1)} %get-tuple-element.56), channel_id=1, source_target_pairs={{0,8},{8,16},{16,24},{1,9},{9,17},{17,25},{2,10},{10,18},{18,26},{... | collective-permute-start | bytes 1179656 | tf_op jit(solution)/shard_map/ppermute | solution.py:50
  154.4 0.7 collective-permute-done.11
  155.1 1.1 fusion.10
  156.2 4.9 %collective-permute-done.12 = bf16[6,16,2048]{2,1,0:T(8,128)(2,1)S(1)} collective-permute-done((bf16[6,16,2048]{2,1,0:T(8,128)(2,1)S(1)}, bf16[6,16,2048]{2,1,0:T(8,128)(2,1)S(1)}, u32[]{:S(2)}, u32[]{:S(2)}) %collective-permute-start.12) | collective-permute-done | bytes 393248 | tf_op jit(solution)/shard_map/ppermute | solution.py:50
  161.3 116.6 %all-reduce.4.cloned.1.call-done = f32[32,2048]{1,0:T(8,128)} async-done(((f32[32,2048]{1,0:T(8,128)}), f32[32,2048]{1,0:T(8,128)}) %all-reduce.4.cloned.1.call-update) | async-done | bytes 262160
  277.9 0.9 dynamic-slice_add_fusion
  279.0 2.6 convolution_add_fusion.1
  281.7 1.5 fusion.8
  (78 shorter events, 2.6 us)
Async XLA Ops:
  7.2 18.8 %copy-start = (bf16[1024,1024]{1,0:T(8,128)(2,1)S(1)}, bf16[1024,1024]{1,0:T(8,128)(2,1)}, u32[]{:S(2)}) copy-start(bf16[1024,1024]{1,0:T(8,128)(2,1)} %param.19) | copy-start | bytes 6291460
  7.2 6.4 %copy-start.10 = (bf16[8,16,1024]{2,1,0:T(8,128)(2,1)S(1)}, bf16[8,16,1024]{2,1,0:T(8,128)(2,1)}, u32[]{:S(2)}) copy-start(bf16[8,16,1024]{2,1,0:T(8,128)(2,1)} %param.15) | copy-start | bytes 786436
  7.2 270.7 %all-reduce.4.cloned.1.call-start = ((), (), s32[]{:S(2)}) async-start(), calls=%async_computation | async-start | bytes 524288
  11.3 2.3 copy-start.8
  14.1 13.8 %collective-permute-start.4 = (bf16[1,1,2048]{2,1,0:T(2,128)(2,1)S(1)}, bf16[1,1,2048]{2,1,0:T(2,128)(2,1)S(1)}, u32[]{:S(2)}, u32[]{:S(2)}) collective-permute-start(bf16[1,1,2048]{2,1,0:T(2,128)(2,1)S(1)} %bitcast.115), channel_id=1, source_target_pairs={{0,1},{1,0},{2,3},{3,2},{4,5},{5,4},{6,7},{7,6},{8,9},{9,8},{10,11... | collective-permute-start | bytes 12296 | tf_op jit(solution)/shard_map/ppermute | solution.py:23
  15.7 30.4 %collective-permute-start = (bf16[6,16,2048]{2,0,1:T(8,128)(2,1)}, bf16[6,16,2048]{2,0,1:T(8,128)(2,1)}, u32[]{:S(2)}, u32[]{:S(2)}) collective-permute-start(bf16[6,16,2048]{2,0,1:T(8,128)(2,1)} %copy.42), channel_id=1, source_target_pairs={{0,8},{8,16},{16,24},{1,9},{9,17},{17,25},{2,10},{10,18},{18,26},{... | collective-permute-start | bytes 1179656 | tf_op jit(solution)/shard_map/ppermute | solution.py:39
  21.9 24.2 %collective-permute-start.1 = (bf16[6,16,2048]{2,0,1:T(8,128)(2,1)}, bf16[6,16,2048]{2,0,1:T(8,128)(2,1)}, u32[]{:S(2)}, u32[]{:S(2)}) collective-permute-start(bf16[6,16,2048]{2,0,1:T(8,128)(2,1)} %copy.43), channel_id=1, source_target_pairs={{8,0},{16,8},{24,16},{9,1},{17,9},{25,17},{10,2},{18,10},{26,18},{... | collective-permute-start | bytes 1179656 | tf_op jit(solution)/shard_map/ppermute | solution.py:42
  28.0 3.7 %collective-permute-start.5 = (bf16[2,1,2048]{2,0,1:T(2,128)(2,1)S(1)}, bf16[2,1,2048]{2,0,1:T(2,128)(2,1)S(1)}, u32[]{:S(2)}, u32[]{:S(2)}) collective-permute-start(bf16[2,1,2048]{2,0,1:T(2,128)(2,1)S(1)} %bitcast.117), channel_id=1, source_target_pairs={{0,2},{1,3},{2,0},{3,1},{4,6},{5,7},{6,4},{7,5},{8,10},{9,11},{10,... | collective-permute-start | bytes 24584 | tf_op jit(solution)/shard_map/ppermute | solution.py:23
  31.8 4.7 %collective-permute-start.6 = (bf16[4,1,2048]{2,0,1:T(4,128)(2,1)S(1)}, bf16[4,1,2048]{2,0,1:T(4,128)(2,1)S(1)}, u32[]{:S(2)}, u32[]{:S(2)}) collective-permute-start(bf16[4,1,2048]{2,0,1:T(4,128)(2,1)S(1)} %reshape.338), channel_id=1, source_target_pairs={{0,4},{1,5},{2,6},{3,7},{4,0},{5,1},{6,2},{7,3},{8,12},{9,13},{10,... | collective-permute-start | bytes 49160 | tf_op jit(solution)/shard_map/ppermute | solution.py:23
  36.6 9.4 %collective-permute-start.7 = (bf16[8,1,2048]{2,0,1:T(8,128)(2,1)S(1)}, bf16[8,1,2048]{2,0,1:T(8,128)(2,1)S(1)}, u32[]{:S(2)}, u32[]{:S(2)}) collective-permute-start(bf16[8,1,2048]{2,0,1:T(8,128)(2,1)S(1)} %reshape.339), channel_id=1, source_target_pairs={{0,8},{1,9},{2,10},{3,11},{4,12},{5,13},{6,14},{7,15},{8,0},{9,1},... | collective-permute-start | bytes 98312 | tf_op jit(solution)/shard_map/ppermute | solution.py:23
  46.0 5.0 %collective-permute-start.8 = (bf16[16,1,2048]{2,0,1:T(8,128)(2,1)S(1)}, bf16[16,1,2048]{2,0,1:T(8,128)(2,1)S(1)}, u32[]{:S(2)}, u32[]{:S(2)}) collective-permute-start(bf16[16,1,2048]{2,0,1:T(8,128)(2,1)S(1)} %get-tuple-element.61), channel_id=1, source_target_pairs={{0,16},{1,17},{2,18},{3,19},{4,20},{5,21},{6,22},{7,23},{8,24},{9,... | collective-permute-start | bytes 196616 | tf_op jit(solution)/shard_map/ppermute | solution.py:23
  47.8 3.3 %collective-permute-start.2 = (bf16[20,6,2048]{2,0,1:T(8,128)(2,1)S(1)}, bf16[20,6,2048]{2,0,1:T(8,128)(2,1)S(1)}, u32[]{:S(2)}, u32[]{:S(2)}) collective-permute-start(bf16[20,6,2048]{2,0,1:T(8,128)(2,1)S(1)} %get-tuple-element.54), channel_id=1, source_target_pairs={{0,1},{1,2},{2,3},{3,4},{4,5},{5,6},{6,7},{8,9},{9,10},{10,11},{11... | collective-permute-start | bytes 1474568 | tf_op jit(solution)/shard_map/ppermute | solution.py:39
  49.6 5.2 %collective-permute-start.3 = (bf16[20,6,2048]{2,0,1:T(8,128)(2,1)S(1)}, bf16[20,6,2048]{2,0,1:T(8,128)(2,1)S(1)}, u32[]{:S(2)}, u32[]{:S(2)}) collective-permute-start(bf16[20,6,2048]{2,0,1:T(8,128)(2,1)S(1)} %get-tuple-element.55), channel_id=1, source_target_pairs={{1,0},{2,1},{3,2},{4,3},{5,4},{6,5},{7,6},{9,8},{10,9},{11,10},{12... | collective-permute-start | bytes 1474568 | tf_op jit(solution)/shard_map/ppermute | solution.py:42
  76.0 2.9 %copy-start.9 = (bf16[592,1024]{0,1:T(8,128)(2,1)S(1)}, bf16[592,1024]{0,1:T(8,128)(2,1)}, u32[]{:S(2)}) copy-start(bf16[592,1024]{0,1:T(8,128)(2,1)} %copy.47) | copy-start | bytes 3637252
  76.0 2.9 %copy-start.11 = (bf16[128,1024]{0,1:T(8,128)(2,1)S(1)}, bf16[128,1024]{0,1:T(8,128)(2,1)}, u32[]{:S(2)}) copy-start(bf16[128,1024]{0,1:T(8,128)(2,1)} %copy.48) | copy-start | bytes 786436
  76.0 6.7 %slice-start = ((s8[4849664]{0:T(1024)(128)(4,1)}), s8[4194304]{0:T(1024)(128)(4,1)S(1)}, s32[]{:S(2)}) async-start(s8[4849664]{0:T(1024)(128)(4,1)} %bitcast.96), calls=%async_computation.1 | async-start | bytes 8388608
  78.9 3.7 %slice-start.1 = ((s8[4849664]{0:T(1024)(128)(4,1)}), s8[655360]{0:T(1024)(128)(4,1)S(1)}, s32[]{:S(2)}) async-start(s8[4849664]{0:T(1024)(128)(4,1)} %bitcast.96), calls=%async_computation.2 | async-start | bytes 1310720
  82.7 1.4 copy-start.13
  84.0 2.4 copy-start.5
  103.2 4.0 %copy-start.1 = (f32[20,28,2048]{2,1,0:T(8,128)S(1)}, f32[20,28,2048]{2,1,0:T(8,128)}, u32[]{:S(2)}) copy-start(f32[20,28,2048]{2,1,0:T(8,128)} %reshape.350) | copy-start | bytes 13762564
  109.2 14.1 %copy-start.12 = (bf16[16,128,64]{1,2,0:T(8,128)(2,1)S(1)}, bf16[16,128,64]{1,2,0:T(8,128)(2,1)}, u32[]{:S(2)}) copy-start(bf16[16,128,64]{1,2,0:T(8,128)(2,1)} %get-tuple-element.67) | copy-start | bytes 786436
  109.5 15.1 %copy-start.6 = (bf16[16,128,592]{1,2,0:T(8,128)(2,1)S(1)}, bf16[16,128,592]{1,2,0:T(8,128)(2,1)}, u32[]{:S(2)}) copy-start(bf16[16,128,592]{1,2,0:T(8,128)(2,1)} %copy-done.5) | copy-start | bytes 7274500
  110.9 15.0 %collective-permute-start.9 = (bf16[20,6,2048]{2,0,1:T(8,128)(2,1)S(1)}, bf16[20,6,2048]{2,0,1:T(8,128)(2,1)S(1)}, u32[]{:S(2)}, u32[]{:S(2)}) collective-permute-start(bf16[20,6,2048]{2,0,1:T(8,128)(2,1)S(1)} %copy.51), channel_id=1, source_target_pairs={{1,0},{2,1},{3,2},{4,3},{5,4},{6,5},{7,6},{9,8},{10,9},{11,10},{12... | collective-permute-start | bytes 1474568 | tf_op jit(solution)/shard_map/ppermute | solution.py:50
  112.2 20.3 %collective-permute-start.10 = (bf16[20,6,2048]{2,0,1:T(8,128)(2,1)}, bf16[20,6,2048]{2,0,1:T(8,128)(2,1)}, u32[]{:S(2)}, u32[]{:S(2)}) collective-permute-start(bf16[20,6,2048]{2,0,1:T(8,128)(2,1)} %copy.53), channel_id=1, source_target_pairs={{0,1},{1,2},{2,3},{3,4},{4,5},{5,6},{6,7},{8,9},{9,10},{10,11},{11... | collective-permute-start | bytes 1474568 | tf_op jit(solution)/shard_map/ppermute | solution.py:50
  141.3 4.3 %copy-start.3 = (f32[592,1024]{1,0:T(8,128)S(1)}, f32[592,1024]{1,0:T(8,128)}, u32[]{:S(2)}) copy-start(f32[592,1024]{1,0:T(8,128)} %copy.50) | copy-start | bytes 7274500
  141.3 4.3 %copy-start.4 = (f32[592,1024]{1,0:T(8,128)S(1)}, f32[592,1024]{1,0:T(8,128)}, u32[]{:S(2)}) copy-start(f32[592,1024]{1,0:T(8,128)} %copy.49) | copy-start | bytes 7274500
  144.1 2.2 copy-start.14
  144.1 10.9 %collective-permute-start.11 = (bf16[6,16,2048]{2,1,0:T(8,128)(2,1)}, bf16[6,16,2048]{2,1,0:T(8,128)(2,1)}, u32[]{:S(2)}, u32[]{:S(2)}) collective-permute-start(bf16[6,16,2048]{2,1,0:T(8,128)(2,1)} %get-tuple-element.57), channel_id=1, source_target_pairs={{8,0},{16,8},{24,16},{9,1},{17,9},{25,17},{10,2},{18,10},{26,18},{... | collective-permute-start | bytes 1179656 | tf_op jit(solution)/shard_map/ppermute | solution.py:50
  146.3 3.4 %copy-start.2 = (f32[20,16,2048]{2,1,0:T(8,128)S(1)}, f32[20,16,2048]{2,1,0:T(8,128)}, u32[]{:S(2)}) copy-start(f32[20,16,2048]{2,1,0:T(8,128)} %scatter-add.15) | copy-start | bytes 7864324
  149.8 11.3 %collective-permute-start.12 = (bf16[6,16,2048]{2,1,0:T(8,128)(2,1)S(1)}, bf16[6,16,2048]{2,1,0:T(8,128)(2,1)S(1)}, u32[]{:S(2)}, u32[]{:S(2)}) collective-permute-start(bf16[6,16,2048]{2,1,0:T(8,128)(2,1)S(1)} %get-tuple-element.56), channel_id=1, source_target_pairs={{0,8},{8,16},{16,24},{1,9},{9,17},{17,25},{2,10},{10,18},{18,26},{... | collective-permute-start | bytes 1179656 | tf_op jit(solution)/shard_map/ppermute | solution.py:50
  279.0 2.7 copy-start.7
Sparse Core Ops, SparseCore 0:
  146.4 131.3 all-reduce.3
